TPU v7x, 256 devices: a whole 4x4x8 slice. The times are simulated.
256 devices in a mesh: ang: 128 (over z, x_lo, y, core), sl: 2 (over x_hi).
Axes of the slice: x: 4 (x_hi: 2, x_lo: 2; x = x_hi * 2 + x_lo), y: 4, z: 8, core: 2. Of those that a mesh axis runs over, the one named last changes fastest.
Arguments:
- projections: float32 [256, 8, 4352], P('ang', 'sl'), may hold values from -6 to 6
- partner: int32 [256], replicated, may hold values from 0 to 255, as said below
- offsets: int32 [256], P('ang'), may hold values from 0 to 192
- angles: float32 [256], replicated, may hold values from 0 to 6.2832, as said below
- coefficients: float32 [2, 8, 4096, 1280], P(None, None, ('ang', 'sl')), may hold values from -6 to 6
Outputs:
- updated: float32 [2, 8, 4096, 1280], P(None, None, ('ang', 'sl'))
- misfit: float32 [256, 8], P('ang', 'sl')
Inputs may be any that keep to these rules, and one draw needn't show every extreme that they name: partner[partner[g]] = g, and g // 2 and partner[g] // 2 differ by 64: a projection's partner lies on the index of ang half the axis away. angles[partner[g]] lies within pi / 128 of angles[g] + pi or angles[g] - pi.
All inputs are finite; a program needn't handle non-finite values.
Results may differ from a plain program's by a relative error of at most 0.0003.
Values sent between devices are 32-bit elements; how exact they have to be, the bound alone decides.
No kernel may reach another device: no remote copies, remote signals or barrier semaphores. Data moves between devices by JAX's collectives and lax.ppermute only.
A program may use at most 64 MiB of HBM per device.

v0:
```python
import functools
import math

import jax
import jax.numpy as jnp
from jax import lax
from jax.sharding import Mesh
from jax.sharding import PartitionSpec as P

W = 8192
HALF = 4096
K = 4096
EXTRA = 256
RAMP = 64
ROWS = 8
ANG = ("ang_0", "ang_1", "ang_2", "ang_3")
ANG_SL = ("ang_0", "ang_1", "ang_2", "ang_3", "sl")


paganin_strength = 16.0
small_eps = 1e-06
highest = lax.Precision.HIGHEST


def from_behind(value, axis, steps):
    count = lax.axis_size(axis)
    pairs = [(source, (source + steps) % count) for source in range(count)]
    return lax.ppermute(value, axis, pairs)


def in_blocks(value, dim, length):
    before, after = (value.shape[:dim], value.shape[dim + 1 :])
    return jnp.moveaxis(value.reshape(*before, length, -1, *after), dim, 0)


def laid_out(parts, dim):
    parts = jnp.moveaxis(parts, 0, dim)
    shape = parts.shape
    return parts.reshape(*shape[:dim], shape[dim] * shape[dim + 1], *shape[dim + 2 :])


def exchange_both(value, axis, axes, splits, concats):
    sizes = [lax.axis_size(a) for a in axes]
    parts = in_blocks(value, splits[0], sizes[0])
    parts = jnp.moveaxis(in_blocks(parts, splits[1] + 1, sizes[1]), 0, 1)
    inside = parts.shape[2:]
    parts = parts.reshape(-1, *inside)
    parts = lax.all_to_all(parts, axis, split_axis=0, concat_axis=0, tiled=True)
    parts = laid_out(parts.reshape(*sizes, *inside), concats[0] + 1)
    return laid_out(parts, concats[1])


def by_axis(value, axes):
    return functools.reduce(lax.psum, axes, value)


def paganin_rows(frequencies):
    row_ids = jnp.arange(ROWS, dtype=jnp.int32)
    row_offset = (row_ids[:, None] - row_ids[None, :]) % ROWS
    cos_table = jnp.cos(
        2.0
        * math.pi
        / ROWS
        * (row_ids[:, None, None] * row_offset[None, :, :] % ROWS).astype(jnp.float32)
    )
    row_freq = jnp.minimum(row_ids, ROWS - row_ids).astype(jnp.float32) / ROWS
    col_freq = frequencies / W
    damping = 1.0 / (
        1.0
        + paganin_strength
        * (col_freq[:, None] * col_freq[:, None] + row_freq[None, :] * row_freq[None, :])
    )
    return jnp.einsum("nq,qij->nij", damping, cos_table, precision=highest) / ROWS


def blend_band(projections, mirrored, offsets):
    position = jnp.arange(EXTRA, dtype=jnp.int32).astype(jnp.float32)
    weight = jnp.clip((position[None, :] - offsets[:, None].astype(jnp.float32)) / RAMP, 0.0, 1.0)
    own_band = projections[:, :, HALF - EXTRA : HALF]
    blended = own_band + weight[:, None, :] * (mirrored - own_band)
    return jnp.concatenate([projections[:, :, : HALF - EXTRA], blended], axis=2)


def spectrum_of(stitched):
    row_count = stitched.shape[0] * stitched.shape[1]
    low_split = W // 128
    outer_count = HALF // low_split
    high_count = K // 128
    folded = stitched.reshape(row_count, outer_count, low_split)
    norm_scale = 1.0 / math.sqrt(HALF)
    outer_ids = jnp.arange(outer_count, dtype=jnp.int32)
    lane_ids = jnp.arange(128, dtype=jnp.int32)
    first_phase = (
        2.0 * math.pi / 128 * (outer_ids[:, None] * lane_ids[None, :] % 128).astype(jnp.float32)
    )
    first_cos = jnp.cos(first_phase) * norm_scale
    first_sin = jnp.sin(first_phase) * norm_scale
    part_real = jnp.einsum("rab,ap->rbp", folded, first_cos, precision=highest)
    part_imag = -jnp.einsum("rab,ap->rbp", folded, first_sin, precision=highest)
    low_ids = jnp.arange(low_split, dtype=jnp.int32)
    twist_phase = 2.0 * math.pi / W * (low_ids[:, None] * lane_ids[None, :]).astype(jnp.float32)
    twist_cos = jnp.cos(twist_phase)
    twist_sin = jnp.sin(twist_phase)
    turned_real = part_real * twist_cos + part_imag * twist_sin
    turned_imag = part_imag * twist_cos - part_real * twist_sin
    high_ids = jnp.arange(high_count, dtype=jnp.int32)
    last_phase = (
        2.0
        * math.pi
        / low_split
        * (low_ids[:, None] * high_ids[None, :] % low_split).astype(jnp.float32)
    )
    last_cos = jnp.cos(last_phase)
    last_sin = jnp.sin(last_phase)
    spec_real = jnp.einsum("rbp,bq->rqp", turned_real, last_cos, precision=highest) + jnp.einsum(
        "rbp,bq->rqp", turned_imag, last_sin, precision=highest
    )
    spec_imag = jnp.einsum("rbp,bq->rqp", turned_imag, last_cos, precision=highest) - jnp.einsum(
        "rbp,bq->rqp", turned_real, last_sin, precision=highest
    )
    out_shape = (stitched.shape[0], stitched.shape[1], K)
    return (spec_real.reshape(out_shape), spec_imag.reshape(out_shape))


def apply_rows(harm_table, coef_part):
    return jnp.einsum("gm,cm->gc", harm_table, coef_part, precision=highest)


def apply_back(harm_table, resid_part):
    return jnp.einsum("gm,gc->cm", harm_table, resid_part, precision=highest)


def shards(projections, partner, offsets, angles, coefficients):
    ang_count = lax.axis_size(ANG)
    sl_count = lax.axis_size("sl")
    ang_index = lax.axis_index(ANG)
    sl_index = lax.axis_index("sl")
    per_dev = projections.shape[0]
    rows_dev = projections.shape[1]
    total_angles = per_dev * ang_count
    block_freqs = coefficients.shape[2]
    harmonics = coefficients.shape[3]
    columns = ROWS * block_freqs
    own_partners = lax.dynamic_slice_in_dim(partner, ang_index * per_dev, per_dev)
    across_dev = (ang_index + ang_count // 2) % ang_count
    partner_slots = own_partners - across_dev * per_dev
    arrived = from_behind(projections[:, :, HALF:], ANG, ang_count // 2)
    mirrored = jnp.flip(jnp.take(arrived, partner_slots, axis=0), axis=2)
    stitched = blend_band(projections, mirrored, offsets)
    spec_real, spec_imag = spectrum_of(stitched)
    spectra = jnp.stack([spec_real, spec_imag])
    regrouped = exchange_both(spectra, ANG_SL, (ANG, "sl"), (3, 3), (1, 2))
    freq_major = regrouped.reshape(2, total_angles, columns)
    freq_base = (ang_index * sl_count + sl_index) * block_freqs
    local_freq = (freq_base + jnp.arange(block_freqs, dtype=jnp.int32)).astype(jnp.float32)
    col_freq = jnp.tile(local_freq, ROWS)
    turn_phase = 2.0 * math.pi / W * col_freq
    turn_cos = jnp.cos(turn_phase)
    turn_sin = jnp.sin(turn_phase)
    own_real = freq_major[0]
    own_imag = freq_major[1]
    pair_real = jnp.take(own_real, partner, axis=0)
    pair_imag = jnp.take(own_imag, partner, axis=0)
    comb_real = own_real + turn_cos * pair_real + turn_sin * pair_imag
    comb_imag = own_imag + turn_sin * pair_real - turn_cos * pair_imag
    rows_matrix = paganin_rows(local_freq)
    full_matrix = jnp.einsum(
        "nij,mn->jmin", rows_matrix, jnp.eye(block_freqs, dtype=jnp.float32)
    ).reshape(columns, columns)
    filt_real = jnp.dot(comb_real, full_matrix, precision=highest)
    filt_imag = jnp.dot(comb_imag, full_matrix, precision=highest)
    ramp_weights = (col_freq + 0.5) / K
    coef_rows = coefficients.reshape(2 * columns, harmonics)
    harm_shift = (jnp.arange(harmonics, dtype=jnp.int32) - harmonics // 2).astype(jnp.float32)
    norm_scale = 1.0 / math.sqrt(harmonics)
    phase_tab = angles[:, None] * harm_shift[None, :]
    tabs = jnp.concatenate([jnp.cos(phase_tab) * norm_scale, jnp.sin(phase_tab) * norm_scale])

    def to_image(coef):
        prod = lax.dot_general(
            tabs, coef, (((1,), (1,)), ((), ())), precision=highest
        )
        cos_part, sin_part = prod[:total_angles], prod[total_angles:]
        real = cos_part[:, :columns] - sin_part[:, columns:]
        imag = cos_part[:, columns:] + sin_part[:, :columns]
        return real, imag

    model_real, model_imag = to_image(coef_rows)
    diff_real = model_real - filt_real
    diff_imag = model_imag - filt_imag
    resid_real = ramp_weights * diff_real
    resid_imag = ramp_weights * diff_imag
    energy = (diff_real * resid_real + diff_imag * resid_imag).reshape(
        total_angles, ROWS, block_freqs
    )
    misfit_table = jnp.sum(energy, axis=2) / K
    stacked = jnp.concatenate(
        [
            jnp.concatenate([resid_real, resid_imag], axis=1),
            jnp.concatenate([resid_imag, -resid_real], axis=1),
        ]
    )
    grad = lax.dot_general(stacked, tabs, (((0,), (0,)), ((), ())), precision=highest)
    image_real, image_imag = to_image(grad)
    curvature = jnp.sum(ramp_weights * (image_real * image_real + image_imag * image_imag))
    grad_norm = jnp.sum(grad * grad)
    table_total = lax.psum(misfit_table, ANG_SL)
    sums = lax.psum(jnp.stack([grad_norm, curvature]), ANG_SL)
    misfit = lax.dynamic_slice(
        table_total, (ang_index * per_dev, sl_index * rows_dev), (per_dev, rows_dev)
    )
    step_size = sums[0] / (sums[1] + small_eps)
    updated = coefficients - step_size * grad.reshape(coefficients.shape)
    return (updated, misfit)


def solution(mesh):
    torus = Mesh(
        mesh.devices.reshape(8, 2, 4, 2, mesh.shape["sl"]),
        ("ang_0", "ang_1", "ang_2", "ang_3", "sl"),
    )
    in_specs = (P(ANG, "sl", None), P(), P(ANG), P(), P(None, None, ANG_SL, None))
    out_specs = (P(None, None, ANG_SL, None), P(ANG, "sl"))
    return jax.shard_map(
        shards, mesh=torus, in_specs=in_specs, out_specs=out_specs, check_vma=False
    )
```

profile of v0, /device:TPU:1, one launch (start us, length us, event | category | flops | bytes accessed | tf_op | source)
XLA Modules:
  0.0 159.2 jit_solution(13492334243215414593)
XLA Ops:
  1.3 7.7 %collective-permute-start = (f32[2,4,256]{2,1,0:T(4,128)S(1)}, f32[2,4,256]{2,1,0:T(4,128)S(1)}, u32[]{:S(2)}, u32[]{:S(2)}) collective-permute-start(f32[2,4,256]{2,1,0:T(4,128)S(1)} %slice.69), channel_id=1, source_target_pairs={{0,128},{2,130},{4,132},{6,134},{8,136},{10,138},{12,140},{14,142}... | collective-permute-start | bytes 24584 | tf_op jit(solution)/shard_map/ppermute | solution.py:28
  11.8 0.8 multiply_bitcast_fusion
  12.7 5.4 %fusion.3 = (f32[256,1280]{1,0:T(8,128)S(1)}, f32[256,1280]{1,0:T(8,128)S(1)}) fusion(f32[1280]{0:T(1024)S(1)} %add_convert_fusion, f32[256]{0:T(256)} %param.10), kind=kLoop, calls=%fused_computation.9 | loop fusion | flops 983040 | bytes 2627584 | tf_op jit(solution)/shard_map/mul | solution.py:177
  22.8 1.9 %copy.46 = f32[128,4,2,4,16]{4,3,2,1,0:T(4,128)} copy(f32[128,4,2,4,16]{0,4,3,2,1:T(8,128)S(1)} %pad_maximum_fusion.4) | data formatting | bytes 524288 | tf_op jit(solution)/shard_map/concatenate
  24.8 3.8 %reshape.226 = f32[256,1,256]{2,1,0:T(1,128)} reshape(f32[256,2,2,4,16]{4,3,2,1,0:T(4,128)} %bitcast.57) | data formatting | bytes 524288
  28.6 11.0 %all-to-all-start = ((f32[256,1,256]{2,1,0:T(1,128)}), f32[256,1,256]{2,1,0:T(1,128)}, u32[]{:S(2)}, u32[]{:S(2)}) async-start(f32[256,1,256]{2,1,0:T(1,128)} %reshape.226), calls=%async_computation | async-start | bytes 524288 | tf_op jit(solution)/shard_map/all_to_all | solution.py:48
  41.3 3.7 %fusion.2 = f32[512,256]{0,1:T(8,128)S(1)} fusion(f32[256,1280]{1,0:T(8,128)} %bitcast.60, f32[256,1280]{1,0:T(8,128)S(1)} %get-tuple-element.16, f32[256,1280]{1,0:T(8,128)S(1)} %get-tuple-element.15), kind=kOutput, calls=%fused_computation.8 | convolution fusion | flops 2013921280 | bytes 4456448 | tf_op jit(solution)/shard_map/dot_general | solution.py:180
  45.0 9.0 %all-to-all-done = f32[256,1,256]{2,1,0:T(1,128)} async-done(((f32[256,1,256]{2,1,0:T(1,128)}), f32[256,1,256]{2,1,0:T(1,128)}, u32[]{:S(2)}, u32[]{:S(2)}) %all-to-all-start) | async-done | bytes 262176 | tf_op jit(solution)/shard_map/all_to_all | solution.py:48
  54.5 2.2 %reduce = f32[256,256]{1,0:T(8,128)S(1)} reduce(f32[256,1,256]{2,1,0:T(1,128)} %all-to-all-done, f32[]{:T(128)} %broadcast.260), dimensions={1}, to_apply=%all_to_all.3.reduce_sub_computation | reduce | bytes 524292 | tf_op jit(solution)/shard_map/all_to_all | solution.py:48
  56.7 2.8 %reshape.227 = f32[256,2,2,4,16]{4,3,2,1,0:T(4,128)} reshape(f32[256,256]{1,0:T(8,128)S(1)} %reduce) | data formatting | bytes 524288
  59.5 2.3 %copy.47 = f32[256,2,2,4,16]{4,0,3,2,1:T(8,128)S(1)} copy(f32[256,2,2,4,16]{4,3,2,1,0:T(4,128)} %reshape.227) | data formatting | bytes 524288 | tf_op jit(solution)/shard_map/all_to_all | solution.py:48
  61.8 1.6 %copy.48 = f32[2,2,128,2,4,16]{5,3,2,4,1,0:T(2,128)S(1)} copy(f32[2,2,128,2,4,16]{5,0,2,4,3,1:T(2,128)S(1)} %bitcast.59) | data formatting | bytes 524288 | tf_op jit(solution)/shard_map/transpose | solution.py:37
  63.4 1.5 fusion.148
  64.9 1.5 copy.52
  66.5 1.5 copy.49
  68.9 1.3 gather_fusion.1
  70.2 1.3 convolution_subtract_fusion
  71.5 1.3 broadcast_multiply_fusion.2
  73.0 2.9 %multiply_reduce_fusion = (f32[]{:T(128)}, f32[256,1280]{1,0:T(8,128)S(1)}) fusion(f32[256,1280]{1,0:T(8,128)S(1)} %get-tuple-element.16, f32[256,1280]{1,0:T(8,128)S(1)} %get-tuple-element.15, f32[256,128]{0,1:T(8,128)S(1)} %get-tuple-element.14, f32[256,128]{0,1:T(8,128)S(1)} %get-tuple-element.19, f32[256,128]{0,1:T(8,128)S(1)} %get-tuple-element.13), kind=kOutput, calls=%fused_computation.11 | convolution fusion | flops 2014969856 | bytes 4325380 | tf_op jit(solution)/shard_map/dot_general | solution.py:203
  75.9 2.7 %fusion = f32[512,256]{0,1:T(8,128)S(1)} fusion(f32[256,1280]{1,0:T(8,128)S(1)} %get-tuple-element.22, f32[256,1280]{1,0:T(8,128)S(1)} %get-tuple-element.16, f32[256,1280]{1,0:T(8,128)S(1)} %get-tuple-element.15), kind=kOutput, calls=%fused_computation.6 | convolution fusion | flops 2013921280 | bytes 4456448 | tf_op jit(solution)/shard_map/dot_general | solution.py:180
  79.4 1.4 pad_maximum_fusion.6
  80.8 72.8 %all-reduce = (f32[2]{0:T(128)S(1)}, f32[256,8]{0,1:T(8,128)S(1)}) all-reduce(f32[2]{0:T(128)S(1)} %pad_maximum_fusion.6, f32[256,8]{0,1:T(8,128)S(1)} %broadcast_multiply_fusion.3), channel_id=1, replica_groups=mesh['ang_0'=8,'ang_1'=2,'ang_2'=4,'ang_3'=2,'sl'=2] {'ang_0','ang_1','a..., use_global_device_ids=true, to_apply=%region_2.4 | all-reduce | flops 2050 | bytes 16400 | tf_op jit(solution)/shard_map/psum | solution.py:208
  155.6 1.5 broadcast_multiply_fusion
  157.3 1.2 sub.100
  (67 shorter events, 13.5 us)
Async XLA Ops:
  1.3 16.8 %collective-permute-start = (f32[2,4,256]{2,1,0:T(4,128)S(1)}, f32[2,4,256]{2,1,0:T(4,128)S(1)}, u32[]{:S(2)}, u32[]{:S(2)}) collective-permute-start(f32[2,4,256]{2,1,0:T(4,128)S(1)} %slice.69), channel_id=1, source_target_pairs={{0,128},{2,130},{4,132},{6,134},{8,136},{10,138},{12,140},{14,142}... | collective-permute-start | bytes 24584 | tf_op jit(solution)/shard_map/ppermute | solution.py:28
  12.7 6.3 %copy-start.3 = (f32[2,4,4352]{2,1,0:T(4,128)S(1)}, f32[2,4,4352]{2,1,0:T(4,128)}, u32[]{:S(2)}) copy-start(f32[2,4,4352]{2,1,0:T(4,128)} %param.7) | copy-start | bytes 417796
  12.7 6.3 %slice-start = ((f32[2,4,4352]{2,1,0:T(4,128)}), f32[2,4,3840]{2,1,0:T(4,128)S(1)}, s32[]{:S(2)}) async-start(f32[2,4,4352]{2,1,0:T(4,128)} %param.7), calls=%async_computation.1 | async-start | bytes 245760 | tf_op jit(solution)/shard_map/slice | solution.py:81
  24.7 15.2 %copy-start.2 = (f32[8,16,8,16]{3,2,1,0:T(8,128)S(1)}, f32[8,16,8,16]{3,2,1,0:T(8,128)}, u32[]{:S(2)}) copy-start(f32[8,16,8,16]{3,2,1,0:T(8,128)} %multiply_bitcast_fusion) | copy-start | bytes 196612
  24.7 16.0 %copy-start.4 = (s32[256]{0:T(256)S(1)}, s32[256]{0:T(256)}, u32[]{:S(2)}) copy-start(s32[256]{0:T(256)} %param.8) | copy-start | bytes 3076
  28.6 25.4 %all-to-all-start = ((f32[256,1,256]{2,1,0:T(1,128)}), f32[256,1,256]{2,1,0:T(1,128)}, u32[]{:S(2)}, u32[]{:S(2)}) async-start(f32[256,1,256]{2,1,0:T(1,128)} %reshape.226), calls=%async_computation | async-start | bytes 524288 | tf_op jit(solution)/shard_map/all_to_all | solution.py:48
  75.9 2.7 %copy-start = (f32[256,1280]{1,0:T(8,128)}, f32[256,1280]{1,0:T(8,128)S(1)}, u32[]{:S(2)}) copy-start(f32[256,1280]{1,0:T(8,128)S(1)} %get-tuple-element.22) | copy-start | bytes 3932164
  155.6 1.7 %copy-start.1 = (f32[2,8,16,1280]{3,2,1,0:T(8,128)S(1)}, f32[2,8,16,1280]{3,2,1,0:T(8,128)}, u32[]{:S(2)}) copy-start(f32[2,8,16,1280]{3,2,1,0:T(8,128)} %param.11) | copy-start | bytes 3932164
where the time goes:
time: 160 us; the launch traced here: 159 us
  blocking collectives  72.8 us (46%)
  local copies, waits for them, and re-layouts  24.7 us (15%)
  starting transfers between devices  18.7 us (12%)
  other arithmetic  16.6 us (10%)
  matrix products  15.1 us (9%)
  waiting for transfers between devices  8.98 us (6%)
  between operations  2.28 us (1%)
    psum x1, blocking collectives, shards(): sums = lax.psum(jnp.stack([grad_norm, curvature]), ANG_SL)  72.8 us
    all_to_all x1, starting transfers between devices, exchange_both(): parts = lax.all_to_all(parts, axis, split_axis=0, concat_axis=0, tiled=True)  11 us
    all_to_all x1, waiting for transfers between devices, exchange_both(): parts = lax.all_to_all(parts, axis, split_axis=0, concat_axis=0, tiled=True)  8.98 us
    ppermute x1, starting transfers between devices, from_behind(): return lax.ppermute(value, axis, pairs)  7.73 us
    unnamed x13, local copies, waits for them, and re-layouts  7.49 us
    dot_general x2, matrix products, to_image(): lax.dot_general(tabs, coef, (((1,), (1,)), ((), ())), precision=highest)  6.45 us
    mul x1, other arithmetic, shards(): jnp.cos(phase_tab) * norm_scale  5.4 us
  transfers between devices with their start and end apart: 2, of which 1 were waited for; matrix products, arithmetic and copies ran while one was open for 9% of the time, Pallas kernels for 0%

commit v1 on v0

--- a/solution.py
+++ b/solution.py
@@ -204,12 +204,14 @@
     image_real, image_imag = to_image(grad)
     curvature = jnp.sum(ramp_weights * (image_real * image_real + image_imag * image_imag))
     grad_norm = jnp.sum(grad * grad)
-    table_total = lax.psum(misfit_table, ANG_SL)
-    sums = lax.psum(jnp.stack([grad_norm, curvature]), ANG_SL)
-    misfit = lax.dynamic_slice(
-        table_total, (ang_index * per_dev, sl_index * rows_dev), (per_dev, rows_dev)
-    )
-    step_size = sums[0] / (sums[1] + small_eps)
+    by_owner = misfit_table.reshape(ang_count, per_dev, sl_count, rows_dev)
+    by_owner = jnp.swapaxes(by_owner, 1, 2).reshape(ang_count * sl_count, per_dev * rows_dev)
+    scalars = jnp.broadcast_to(jnp.stack([grad_norm, curvature])[None], (ang_count * sl_count, 2))
+    payload = jnp.concatenate([by_owner, scalars], axis=1)
+    received = lax.all_to_all(payload, ANG_SL, 0, 0, tiled=True)
+    totals = jnp.sum(received, axis=0)
+    misfit = totals[: per_dev * rows_dev].reshape(per_dev, rows_dev)
+    step_size = totals[per_dev * rows_dev] / (totals[per_dev * rows_dev + 1] + small_eps)
     updated = coefficients - step_size * grad.reshape(coefficients.shape)
     return (updated, misfit)
 

time: 160 us -> 108 us (0.68)
  blocking collectives: 72.8 us -> 18.8 us
    psum x1 -> x0, blocking collectives: 72.8 us -> none  [shards(): sums = lax.psum(jnp.stack([grad_norm, curvature]), ANG_SL)]
    all_to_all x0 -> x1, blocking collectives: none -> 18.8 us  [shards(): received = lax.all_to_all(payload, ANG_SL, 0, 0, tiled=True)]
    unnamed x13 -> x18, local copies, waits for them, and re-layouts: 7.49 us -> 7.06 us
  transfers between devices with their start and end apart: 2 -> 2, of which waited for: 1 -> 1; matrix products, arithmetic and copies ran while one was open for 9% -> 13% of each run, Pallas kernels for 0% -> 0%
where the time goes in v1:
time: 108 us; the launch traced here: 107 us
  local copies, waits for them, and re-layouts  25.6 us (24%)
  blocking collectives  18.8 us (17%)
  starting transfers between devices  18.7 us (17%)
  other arithmetic  16.8 us (16%)
  matrix products  15.8 us (15%)
  waiting for transfers between devices  8.89 us (8%)
  between operations  2.28 us (2%)
    all_to_all x1, blocking collectives, shards(): received = lax.all_to_all(payload, ANG_SL, 0, 0, tiled=True)  18.8 us
    all_to_all x1, starting transfers between devices, exchange_both(): parts = lax.all_to_all(parts, axis, split_axis=0, concat_axis=0, tiled=True)  11 us
    all_to_all x1, waiting for transfers between devices, exchange_both(): parts = lax.all_to_all(parts, axis, split_axis=0, concat_axis=0, tiled=True)  8.88 us
    ppermute x1, starting transfers between devices, from_behind(): return lax.ppermute(value, axis, pairs)  7.73 us
    unnamed x18, local copies, waits for them, and re-layouts  7.06 us
    dot_general x2, matrix products, to_image(): lax.dot_general(tabs, coef, (((1,), (1,)), ((), ())), precision=highest)  6.44 us
    mul x1, other arithmetic, shards(): jnp.cos(phase_tab) * norm_scale  5.4 us
    slice x2, local copies, waits for them, and re-layouts, shards(): own_imag = freq_major[1]  2.98 us
  transfers between devices with their start and end apart: 2, of which 1 were waited for; matrix products, arithmetic and copies ran while one was open for 13% of the time, Pallas kernels for 0%

profile of v1, /device:TPU:1, one launch (start us, length us, event | category | flops | bytes accessed | tf_op | source)
XLA Modules:
  0.0 107.0 jit_solution(15330252725112726194)
XLA Ops:
  1.3 7.7 %collective-permute-start = (f32[2,4,256]{2,1,0:T(4,128)S(1)}, f32[2,4,256]{2,1,0:T(4,128)S(1)}, u32[]{:S(2)}, u32[]{:S(2)}) collective-permute-start(f32[2,4,256]{2,1,0:T(4,128)S(1)} %slice.72), channel_id=1, source_target_pairs={{0,128},{2,130},{4,132},{6,134},{8,136},{10,138},{12,140},{14,142}... | collective-permute-start | bytes 24584 | tf_op jit(solution)/shard_map/ppermute | solution.py:28
  11.8 0.8 multiply_bitcast_fusion
  12.7 5.4 %fusion.3 = (f32[256,1280]{1,0:T(8,128)S(1)}, f32[256,1280]{1,0:T(8,128)S(1)}) fusion(f32[1280]{0:T(1024)S(1)} %add_convert_fusion, f32[256]{0:T(256)} %param.10), kind=kLoop, calls=%fused_computation.9 | loop fusion | flops 983040 | bytes 2627584 | tf_op jit(solution)/shard_map/mul | solution.py:177
  22.8 1.9 %copy.70 = f32[128,4,2,4,16]{4,3,2,1,0:T(4,128)} copy(f32[128,4,2,4,16]{0,4,3,2,1:T(8,128)S(1)} %pad_maximum_fusion.4) | data formatting | bytes 524288 | tf_op jit(solution)/shard_map/concatenate
  24.7 3.8 %reshape.242 = f32[256,1,256]{2,1,0:T(1,128)} reshape(f32[256,2,2,4,16]{4,3,2,1,0:T(4,128)} %bitcast.62) | data formatting | bytes 524288
  28.6 11.0 %all-to-all-start = ((f32[256,1,256]{2,1,0:T(1,128)}), f32[256,1,256]{2,1,0:T(1,128)}, u32[]{:S(2)}, u32[]{:S(2)}) async-start(f32[256,1,256]{2,1,0:T(1,128)} %reshape.242), calls=%async_computation | async-start | bytes 524288 | tf_op jit(solution)/shard_map/all_to_all | solution.py:48
  41.3 3.7 %fusion.2 = f32[512,256]{0,1:T(8,128)S(1)} fusion(f32[256,1280]{1,0:T(8,128)} %bitcast.65, f32[256,1280]{1,0:T(8,128)S(1)} %get-tuple-element.12, f32[256,1280]{1,0:T(8,128)S(1)} %get-tuple-element.11), kind=kOutput, calls=%fused_computation.8 | convolution fusion | flops 2013921280 | bytes 4456448 | tf_op jit(solution)/shard_map/dot_general | solution.py:180
  45.0 8.9 %all-to-all-done = f32[256,1,256]{2,1,0:T(1,128)} async-done(((f32[256,1,256]{2,1,0:T(1,128)}), f32[256,1,256]{2,1,0:T(1,128)}, u32[]{:S(2)}, u32[]{:S(2)}) %all-to-all-start) | async-done | bytes 262176 | tf_op jit(solution)/shard_map/all_to_all | solution.py:48
  54.4 2.2 %reduce.1 = f32[256,256]{1,0:T(8,128)S(1)} reduce(f32[256,1,256]{2,1,0:T(1,128)} %all-to-all-done, f32[]{:T(128)} %broadcast.266), dimensions={1}, to_apply=%all_to_all.9.reduce_sub_computation | reduce | bytes 524292 | tf_op jit(solution)/shard_map/all_to_all | solution.py:48
  56.6 2.8 %reshape.243 = f32[256,2,2,4,16]{4,3,2,1,0:T(4,128)} reshape(f32[256,256]{1,0:T(8,128)S(1)} %reduce.1) | data formatting | bytes 524288
  59.4 2.3 %copy.71 = f32[256,2,2,4,16]{4,0,3,2,1:T(8,128)S(1)} copy(f32[256,2,2,4,16]{4,3,2,1,0:T(4,128)} %reshape.243) | data formatting | bytes 524288 | tf_op jit(solution)/shard_map/all_to_all | solution.py:48
  61.7 1.6 %copy.72 = f32[2,2,128,2,4,16]{5,3,2,4,1,0:T(2,128)S(1)} copy(f32[2,2,128,2,4,16]{5,0,2,4,3,1:T(2,128)S(1)} %bitcast.64) | data formatting | bytes 524288 | tf_op jit(solution)/shard_map/transpose | solution.py:37
  63.3 1.5 %fusion.148 = (f32[1,256,2,4,16]{4,1,3,0,2:T(8,128)}, f32[1,256,2,4,16]{4,1,3,0,2:T(8,128)}) fusion(f32[2,256,2,4,16]{4,1,3,0,2:T(8,128)S(1)} %bitcast.63), kind=kLoop, calls=%fused_computation.202 | loop fusion | bytes 524288 | tf_op jit(solution)/shard_map/slice | solution.py:161
  64.8 1.5 %copy.76 = f32[1,256,2,4,16]{1,4,3,2,0:T(8,128)S(1)} copy(f32[1,256,2,4,16]{4,1,3,0,2:T(8,128)} %get-tuple-element.5) | data formatting | bytes 262144 | tf_op jit(solution)/shard_map/slice | solution.py:161
  66.4 1.5 %copy.73 = f32[1,256,2,4,16]{1,4,3,2,0:T(8,128)S(1)} copy(f32[1,256,2,4,16]{4,1,3,0,2:T(8,128)} %get-tuple-element.6) | data formatting | bytes 262144 | tf_op jit(solution)/shard_map/slice | solution.py:160
  68.8 1.3 %gather_fusion.1 = f32[256,128]{1,0:T(8,128)} fusion(f32[256,128]{1,0:T(8,128)S(1)} %copy.75, s32[1024]{0:T(1024)S(1)} %pad_clamp_fusion), kind=kCustom, calls=%fused_computation.clone | custom fusion | bytes 263168 | tf_op jit(solution)/shard_map/jit(_take)/gather | solution.py:162
  70.1 1.3 %convolution_subtract_fusion = f32[256,128]{0,1:T(8,128)S(1)} fusion(f32[128,128]{1,0:T(8,128)} %reshape.200, f32[512,256]{0,1:T(8,128)S(1)} %fusion.2, f32[256,128]{1,0:T(8,128)S(1)} %copy.77, f32[256,128]{1,0:T(8,128)S(1)} %gather_fusion.2, f32[256,128]{1,0:T(8,128)} %gather_fusion.1, f32[128]{0:T(128)S(1)} %sin.36, f32[128]{0:T(128)S(1)} %cos.39, ...), kind=kOutput, calls=%fused_computation.13 | convolution fusion | flops 50593792 | bytes 853248 | tf_op jit(solution)/shard_map/dot_general | solution.py:171
  71.4 2.0 %broadcast_multiply_fusion.2 = (f32[256,128]{0,1:T(8,128)}, f32[256,128]{0,1:T(8,128)}, f32[256,128]{0,1:T(8,128)}, f32[256,128]{0,1:T(8,128)S(1)}) fusion(f32[128]{0:T(128)S(1)} %div.52, f32[256,128]{0,1:T(8,128)S(1)} %convolution_subtract_fusion, f32[128,128]{1,0:T(8,128)} %reshape.200, f32[256,128]{1,0:T(8,128)S(1)} %copy.75, ...), kind=kOutput, calls=%fused_computation.62 | convolution fusion | flops 50692096 | bytes 1378048 | tf_op jit(solution)/shard_map/dot_general | solution.py:170
  74.5 2.9 %multiply_reduce_fusion = (f32[]{:T(128)}, f32[256,1280]{1,0:T(8,128)S(1)}) fusion(f32[256,1280]{1,0:T(8,128)S(1)} %get-tuple-element.12, f32[256,1280]{1,0:T(8,128)S(1)} %get-tuple-element.11, f32[256,128]{0,1:T(8,128)S(1)} %copy-done.4, f32[256,128]{0,1:T(8,128)S(1)} %copy-done.5, f32[256,128]{0,1:T(8,128)S(1)} %copy-done.3), kind=kOutput, calls=%fused_computation.11 | convolution fusion | flops 2014969856 | bytes 4325380 | tf_op jit(solution)/shard_map/dot_general | solution.py:203
  77.4 2.7 %fusion = f32[512,256]{0,1:T(8,128)S(1)} fusion(f32[256,1280]{1,0:T(8,128)S(1)} %get-tuple-element.18, f32[256,1280]{1,0:T(8,128)S(1)} %get-tuple-element.12, f32[256,1280]{1,0:T(8,128)S(1)} %get-tuple-element.11), kind=kOutput, calls=%fused_computation.6 | convolution fusion | flops 2013921280 | bytes 4456448 | tf_op jit(solution)/shard_map/dot_general | solution.py:180
  80.9 1.4 %pad_maximum_fusion.7 = f32[10]{0:T(128)S(1)} fusion(f32[1]{0:T(128)} %bitcast.23, f32[1]{0:T(128)} %bitcast.22), kind=kLoop, calls=%fused_computation.157 | loop fusion | flops 10 | bytes 48 | tf_op jit(solution)/shard_map/stack | solution.py:209
  82.3 18.8 %all_to_all.14 = f32[256,1,10]{2,1,0:T(1,128)S(1)} all-to-all(f32[256,1,10]{2,1,0:T(1,128)S(1)} %bitcast.70), channel_id=1, replica_groups=mesh['ang_0'=8,'ang_1'=2,'ang_2'=4,'ang_3'=2,'sl'=2] {'ang_0','ang_1','a..., dimensions={0} | all-to-all | bytes 20480 | tf_op jit(solution)/shard_map/all_to_all | solution.py:211
  104.1 1.5 %broadcast_multiply_fusion = f32[256,1280]{1,0:T(8,128)S(1)} fusion(f32[256,1280]{1,0:T(8,128)} %copy-done, f32[]{:T(128)} %bitcast.26), kind=kLoop, calls=%fused_computation.21 | loop fusion | flops 327680 | bytes 2621444 | tf_op jit(solution)/shard_map/mul | solution.py:215
  105.8 1.2 %sub.100 = f32[2,8,16,1280]{3,2,1,0:T(8,128)} subtract(f32[2,8,16,1280]{3,2,1,0:T(8,128)S(1)} %copy-done.1, f32[2,8,16,1280]{3,2,1,0:T(8,128)S(1)} %bitcast.66) | non-fusion elementwise | flops 327680 | bytes 3932160 | tf_op jit(solution)/shard_map/sub | solution.py:215
  (78 shorter events, 14.7 us)
Async XLA Ops:
  1.3 16.8 %collective-permute-start = (f32[2,4,256]{2,1,0:T(4,128)S(1)}, f32[2,4,256]{2,1,0:T(4,128)S(1)}, u32[]{:S(2)}, u32[]{:S(2)}) collective-permute-start(f32[2,4,256]{2,1,0:T(4,128)S(1)} %slice.72), channel_id=1, source_target_pairs={{0,128},{2,130},{4,132},{6,134},{8,136},{10,138},{12,140},{14,142}... | collective-permute-start | bytes 24584 | tf_op jit(solution)/shard_map/ppermute | solution.py:28
  12.7 6.3 %copy-start.6 = (f32[2,4,4352]{2,1,0:T(4,128)S(1)}, f32[2,4,4352]{2,1,0:T(4,128)}, u32[]{:S(2)}) copy-start(f32[2,4,4352]{2,1,0:T(4,128)} %param.7) | copy-start | bytes 417796
  12.7 6.3 %slice-start = ((f32[2,4,4352]{2,1,0:T(4,128)}), f32[2,4,3840]{2,1,0:T(4,128)S(1)}, s32[]{:S(2)}) async-start(f32[2,4,4352]{2,1,0:T(4,128)} %param.7), calls=%async_computation.2 | async-start | bytes 245760 | tf_op jit(solution)/shard_map/slice | solution.py:81
  24.7 15.2 %copy-start.2 = (f32[8,16,8,16]{3,2,1,0:T(8,128)S(1)}, f32[8,16,8,16]{3,2,1,0:T(8,128)}, u32[]{:S(2)}) copy-start(f32[8,16,8,16]{3,2,1,0:T(8,128)} %multiply_bitcast_fusion) | copy-start | bytes 196612
  24.7 16.0 %copy-start.7 = (s32[256]{0:T(256)S(1)}, s32[256]{0:T(256)}, u32[]{:S(2)}) copy-start(s32[256]{0:T(256)} %param.8) | copy-start | bytes 3076
  28.6 25.3 %all-to-all-start = ((f32[256,1,256]{2,1,0:T(1,128)}), f32[256,1,256]{2,1,0:T(1,128)}, u32[]{:S(2)}, u32[]{:S(2)}) async-start(f32[256,1,256]{2,1,0:T(1,128)} %reshape.242), calls=%async_computation | async-start | bytes 524288 | tf_op jit(solution)/shard_map/all_to_all | solution.py:48
  73.4 0.9 copy-start.3
  73.4 1.0 copy-start.4
  73.4 1.0 copy-start.5
  77.4 2.7 %copy-start = (f32[256,1280]{1,0:T(8,128)}, f32[256,1280]{1,0:T(8,128)S(1)}, u32[]{:S(2)}) copy-start(f32[256,1280]{1,0:T(8,128)S(1)} %get-tuple-element.18) | copy-start | bytes 3932164
  104.1 1.7 %copy-start.1 = (f32[2,8,16,1280]{3,2,1,0:T(8,128)S(1)}, f32[2,8,16,1280]{3,2,1,0:T(8,128)}, u32[]{:S(2)}) copy-start(f32[2,8,16,1280]{3,2,1,0:T(8,128)} %param.11) | copy-start | bytes 3932164

commit v2 on v1

--- a/solution.py
+++ b/solution.py
@@ -118,8 +118,7 @@
     spec_imag = jnp.einsum("rbp,bq->rqp", turned_imag, last_cos, precision=highest) - jnp.einsum(
         "rbp,bq->rqp", turned_real, last_sin, precision=highest
     )
-    out_shape = (stitched.shape[0], stitched.shape[1], K)
-    return (spec_real.reshape(out_shape), spec_imag.reshape(out_shape))
+    return (spec_real, spec_imag)
 
 
 def apply_rows(harm_table, coef_part):
@@ -149,8 +148,13 @@
     stitched = blend_band(projections, mirrored, offsets)
     spec_real, spec_imag = spectrum_of(stitched)
     spectra = jnp.stack([spec_real, spec_imag])
-    regrouped = exchange_both(spectra, ANG_SL, (ANG, "sl"), (3, 3), (1, 2))
-    freq_major = regrouped.reshape(2, total_angles, columns)
+    dev_count = ang_count * sl_count
+    lane_split = 128 // block_freqs
+    spectra = spectra.reshape(2, per_dev * rows_dev, K // 128, lane_split, block_freqs)
+    payload = spectra.transpose(2, 3, 0, 1, 4).reshape(dev_count, -1)
+    received = lax.all_to_all(payload, ANG_SL, 0, 0, tiled=True)
+    received = received.reshape(ang_count, sl_count, 2, per_dev, rows_dev * block_freqs)
+    freq_major = received.transpose(2, 0, 3, 1, 4).reshape(2, total_angles, columns)
     freq_base = (ang_index * sl_count + sl_index) * block_freqs
     local_freq = (freq_base + jnp.arange(block_freqs, dtype=jnp.int32)).astype(jnp.float32)
     col_freq = jnp.tile(local_freq, ROWS)
@@ -159,8 +163,11 @@
     turn_sin = jnp.sin(turn_phase)
     own_real = freq_major[0]
     own_imag = freq_major[1]
-    pair_real = jnp.take(own_real, partner, axis=0)
-    pair_imag = jnp.take(own_imag, partner, axis=0)
+    swap = (partner[:, None] == jnp.arange(total_angles, dtype=jnp.int32)[None, :]).astype(jnp.float32)
+    own_both = jnp.concatenate([own_real, own_imag], axis=1)
+    pair_both = jnp.dot(swap, own_both, precision=highest)
+    pair_real = pair_both[:, :columns]
+    pair_imag = pair_both[:, columns:]
     comb_real = own_real + turn_cos * pair_real + turn_sin * pair_imag
     comb_imag = own_imag + turn_sin * pair_real - turn_cos * pair_imag
     rows_matrix = paganin_rows(local_freq)

time: 108 us -> 98.6 us (0.913)
  local copies, waits for them, and re-layouts: 25.6 us -> 18.7 us
  other arithmetic: 16.8 us -> 15.6 us
  matrix products: 15.8 us -> 14.7 us
    unnamed x18 -> x14, local copies, waits for them, and re-layouts: 7.06 us -> 0.39 us
    transpose x1, local copies, waits for them, and re-layouts: 1.62 us -> 4.01 us  [shards(): payload = spectra.transpose(2, 3, 0, 1, 4).reshape(dev_count, -1)]
    transpose x1, other arithmetic: 0.02 us -> 2.11 us  [shards(): payload = spectra.transpose(2, 3, 0, 1, 4).reshape(dev_count, -1)]
    gather x2 -> x0, local copies, waits for them, and re-layouts: 2.08 us -> none  [the longest x1 1.34 us: shards(): pair_real = jnp.take(own_real, partner, axis=0)]
    concatenate x1 -> x0, local copies, waits for them, and re-layouts: 1.95 us -> none
    slice x2, local copies, waits for them, and re-layouts: 2.98 us -> 1.72 us  [shards(): own_imag = freq_major[1]]
    all_to_all x2 -> x1, local copies, waits for them, and re-layouts: 2.78 us -> 3.01 us  [shards(): received = lax.all_to_all(payload, ANG_SL, 0, 0, tiled=True)]
  transfers between devices with their start and end apart: 2 -> 2, of which waited for: 1 -> 1; matrix products, arithmetic and copies ran while one was open for 13% -> 12% of each run, Pallas kernels for 0% -> 0%
where the time goes in v2:
time: 98.6 us; the launch traced here: 98 us
  blocking collectives  18.8 us (19%)
  local copies, waits for them, and re-layouts  18.7 us (19%)
  starting transfers between devices  18.6 us (19%)
  other arithmetic  15.6 us (16%)
  matrix products  14.7 us (15%)
  waiting for transfers between devices  9.47 us (10%)
  between operations  2.2 us (2%)
    all_to_all x1, blocking collectives, shards(): received = lax.all_to_all(payload, ANG_SL, 0, 0, tiled=True)  18.8 us
    all_to_all x1, starting transfers between devices, shards(): received = lax.all_to_all(payload, ANG_SL, 0, 0, tiled=True)  10.9 us
    all_to_all x1, waiting for transfers between devices, shards(): received = lax.all_to_all(payload, ANG_SL, 0, 0, tiled=True)  9.47 us
    ppermute x1, starting transfers between devices, from_behind(): return lax.ppermute(value, axis, pairs)  7.73 us
    dot_general x2, matrix products, to_image(): lax.dot_general(tabs, coef, (((1,), (1,)), ((), ())), precision=highest)  7.01 us
    mul x1, other arithmetic, shards(): jnp.cos(phase_tab) * norm_scale  5.4 us
    transpose x1, local copies, waits for them, and re-layouts, shards(): payload = spectra.transpose(2, 3, 0, 1, 4).reshape(dev_count, -1)  4.01 us
    all_to_all x1, local copies, waits for them, and re-layouts, shards(): received = lax.all_to_all(payload, ANG_SL, 0, 0, tiled=True)  3.01 us
  transfers between devices with their start and end apart: 2, of which 1 were waited for; matrix products, arithmetic and copies ran while one was open for 12% of the time, Pallas kernels for 0%

profile of v2, /device:TPU:1, one launch (start us, length us, event | category | flops | bytes accessed | tf_op | source)
XLA Modules:
  0.0 98.0 jit_solution(481471903640869956)
XLA Ops:
  0.6 0.7 slice.72
  1.3 7.7 %collective-permute-start = (f32[2,4,256]{2,1,0:T(4,128)S(1)}, f32[2,4,256]{2,1,0:T(4,128)S(1)}, u32[]{:S(2)}, u32[]{:S(2)}) collective-permute-start(f32[2,4,256]{2,1,0:T(4,128)S(1)} %slice.72), channel_id=1, source_target_pairs={{0,128},{2,130},{4,132},{6,134},{8,136},{10,138},{12,140},{14,142}... | collective-permute-start | bytes 24584 | tf_op jit(solution)/shard_map/ppermute | solution.py:28
  10.0 5.4 %fusion.3 = (f32[256,1280]{1,0:T(8,128)S(1)}, f32[256,1280]{1,0:T(8,128)S(1)}) fusion(f32[1280]{0:T(1024)S(1)} %add_convert_fusion, f32[256]{0:T(256)} %param.8), kind=kLoop, calls=%fused_computation.7 | loop fusion | flops 983040 | bytes 2627584 | tf_op jit(solution)/shard_map/mul | solution.py:184
  20.0 1.0 %copy.46 = f32[8,32,128]{1,2,0:T(8,128)} copy(f32[8,32,128]{2,1,0:T(8,128)S(1)} %fusion.5) | data formatting | bytes 262144 | tf_op jit(solution)/shard_map/sub | solution.py:118
  21.0 2.1 %maximum_bitcast_fusion = f32[32,8,2,8,16]{0,4,1,3,2:T(8,128)} fusion(f32[1,8,32,8,16]{2,4,3,1,0:T(8,128)} %bitcast.62, f32[1,8,32,8,16]{2,4,3,1,0:T(8,128)S(1)} %bitcast.60), kind=kLoop, calls=%fused_computation.19 | loop fusion | flops 65536 | bytes 524288 | tf_op jit(solution)/shard_map/transpose | solution.py:154
  23.1 4.0 %copy.47 = f32[32,8,2,8,16]{4,3,2,1,0:T(8,128)} copy(f32[32,8,2,8,16]{0,4,1,3,2:T(8,128)} %maximum_bitcast_fusion) | data formatting | bytes 524288 | tf_op jit(solution)/shard_map/transpose | solution.py:154
  27.1 3.0 %all_to_all.16 = f32[256,1,256]{2,1,0:T(1,128)} reshape(f32[32,8,2,8,16]{4,3,2,1,0:T(8,128)} %copy.47) | data formatting | bytes 524288 | tf_op jit(solution)/shard_map/all_to_all | solution.py:155
  30.1 10.9 %all-to-all-start = ((f32[256,1,256]{2,1,0:T(1,128)}), f32[256,1,256]{2,1,0:T(1,128)}, u32[]{:S(2)}, u32[]{:S(2)}) async-start(f32[256,1,256]{2,1,0:T(1,128)} %all_to_all.16), calls=%async_computation | async-start | bytes 524288 | tf_op jit(solution)/shard_map/all_to_all | solution.py:155
  41.6 4.5 %fusion.2 = f32[512,256]{0,1:T(8,128)} fusion(f32[256,1280]{1,0:T(8,128)} %bitcast.58, f32[256,1280]{1,0:T(8,128)S(1)} %get-tuple-element.9, f32[256,1280]{1,0:T(8,128)S(1)} %get-tuple-element.8), kind=kOutput, calls=%fused_computation.6 | convolution fusion | flops 2013921280 | bytes 4456448 | tf_op jit(solution)/shard_map/dot_general | solution.py:187
  46.1 9.5 %all-to-all-done = f32[256,1,256]{2,1,0:T(1,128)} async-done(((f32[256,1,256]{2,1,0:T(1,128)}), f32[256,1,256]{2,1,0:T(1,128)}, u32[]{:S(2)}, u32[]{:S(2)}) %all-to-all-start) | async-done | bytes 262176 | tf_op jit(solution)/shard_map/all_to_all | solution.py:155
  55.6 1.6 %reduce.1 = f32[256,256]{1,0:T(8,128)S(1)} reduce(f32[256,1,256]{2,1,0:T(1,128)} %all-to-all-done, f32[]{:T(128)} %constant.146), dimensions={1}, to_apply=%all_to_all.13.reduce_sub_computation | reduce | bytes 524292 | tf_op jit(solution)/shard_map/all_to_all | solution.py:155
  57.5 0.9 fusion.148
  58.3 0.8 copy.50
  59.2 1.1 %squeeze.9 = f32[256,128]{1,0:T(8,128)S(1)} reshape(f32[1,128,2,2,64]{4,3,2,1,0:T(2,128)} %copy.50) | data formatting | bytes 262144 | tf_op jit(solution)/shard_map/squeeze | solution.py:165
  60.3 1.8 %copy.49 = f32[1,128,2,2,64]{4,3,2,1,0:T(2,128)} copy(f32[1,128,2,2,64]{4,2,0,3,1:T(2,128)} %get-tuple-element.5) | data formatting | bytes 262144 | tf_op jit(solution)/shard_map/slice | solution.py:164
  62.1 1.1 %squeeze.8 = f32[256,128]{1,0:T(8,128)S(1)} reshape(f32[1,128,2,2,64]{4,3,2,1,0:T(2,128)} %copy.49) | data formatting | bytes 262144 | tf_op jit(solution)/shard_map/squeeze | solution.py:164
  63.9 1.0 %broadcast_multiply_fusion.2 = (f32[256,128]{0,1:T(8,128)S(1)}, f32[256,128]{0,1:T(8,128)}, f32[256,128]{0,1:T(8,128)}, f32[256,128]{0,1:T(8,128)S(1)}) fusion(f32[128]{0:T(128)S(1)} %div.52, f32[256,128]{0,1:T(8,128)S(1)} %convolution_subtract_fusion, f32[128,128]{1,0:T(8,128)S(1)} %reshape.193, f32[256,128]{1,0:T(8,128)S(1)} %squeeze.8, ...), kind=kOutput, calls=%fused_computation.63 | convolution fusion | flops 50626560 | bytes 1377792 | tf_op jit(solution)/shard_map/dot_general | solution.py:177
  65.8 2.9 %multiply_reduce_fusion = (f32[]{:T(128)}, f32[256,1280]{1,0:T(8,128)S(1)}) fusion(f32[256,1280]{1,0:T(8,128)S(1)} %get-tuple-element.9, f32[256,1280]{1,0:T(8,128)S(1)} %get-tuple-element.8, f32[256,128]{0,1:T(8,128)S(1)} %copy-done.3, f32[256,128]{0,1:T(8,128)S(1)} %copy-done.4, f32[256,128]{0,1:T(8,128)S(1)} %get-tuple-element.6), kind=kOutput, calls=%fused_computation.9 | convolution fusion | flops 2014969856 | bytes 4325380 | tf_op jit(solution)/shard_map/dot_general | solution.py:210
  68.8 2.5 %fusion = f32[512,256]{0,1:T(8,128)S(1)} fusion(f32[256,1280]{1,0:T(8,128)S(1)} %get-tuple-element.15, f32[256,1280]{1,0:T(8,128)S(1)} %get-tuple-element.9, f32[256,1280]{1,0:T(8,128)S(1)} %get-tuple-element.8), kind=kOutput, calls=%fused_computation.4 | convolution fusion | flops 2013921280 | bytes 4456448 | tf_op jit(solution)/shard_map/dot_general | solution.py:187
  71.3 0.8 fusion.22
  72.1 1.4 %pad_maximum_fusion.6 = f32[10]{0:T(128)S(1)} fusion(f32[1]{0:T(128)} %bitcast.18, f32[1]{0:T(128)} %bitcast.17), kind=kLoop, calls=%fused_computation.153 | loop fusion | flops 10 | bytes 48 | tf_op jit(solution)/shard_map/stack | solution.py:216
  73.5 18.8 %all_to_all.19 = f32[256,1,10]{2,1,0:T(1,128)S(1)} all-to-all(f32[256,1,10]{2,1,0:T(1,128)S(1)} %bitcast.64), channel_id=1, replica_groups=mesh['ang_0'=8,'ang_1'=2,'ang_2'=4,'ang_3'=2,'sl'=2] {'ang_0','ang_1','a..., dimensions={0} | all-to-all | bytes 20480 | tf_op jit(solution)/shard_map/all_to_all | solution.py:218
  95.1 1.5 %broadcast_multiply_fusion = f32[256,1280]{1,0:T(8,128)S(1)} fusion(f32[256,1280]{1,0:T(8,128)} %copy-done, f32[]{:T(128)} %bitcast.21), kind=kLoop, calls=%fused_computation.20 | loop fusion | flops 327680 | bytes 2621444 | tf_op jit(solution)/shard_map/mul | solution.py:222
  96.8 1.2 %sub.100 = f32[2,8,16,1280]{3,2,1,0:T(8,128)} subtract(f32[2,8,16,1280]{3,2,1,0:T(8,128)S(1)} %copy-done.1, f32[2,8,16,1280]{3,2,1,0:T(8,128)S(1)} %bitcast.59) | non-fusion elementwise | flops 327680 | bytes 3932160 | tf_op jit(solution)/shard_map/sub | solution.py:222
  (65 shorter events, 9.6 us)
Async XLA Ops:
  1.3 14.6 %collective-permute-start = (f32[2,4,256]{2,1,0:T(4,128)S(1)}, f32[2,4,256]{2,1,0:T(4,128)S(1)}, u32[]{:S(2)}, u32[]{:S(2)}) collective-permute-start(f32[2,4,256]{2,1,0:T(4,128)S(1)} %slice.72), channel_id=1, source_target_pairs={{0,128},{2,130},{4,132},{6,134},{8,136},{10,138},{12,140},{14,142}... | collective-permute-start | bytes 24584 | tf_op jit(solution)/shard_map/ppermute | solution.py:28
  10.0 5.4 %copy-start.6 = (s32[256]{0:T(256)S(1)}, s32[256]{0:T(256)}, u32[]{:S(2)}) copy-start(s32[256]{0:T(256)} %param.6) | copy-start | bytes 3076
  10.0 6.7 %copy-start.5 = (f32[2,4,4352]{2,1,0:T(4,128)S(1)}, f32[2,4,4352]{2,1,0:T(4,128)}, u32[]{:S(2)}) copy-start(f32[2,4,4352]{2,1,0:T(4,128)} %param.5) | copy-start | bytes 417796
  10.0 6.7 %slice-start = ((f32[2,4,4352]{2,1,0:T(4,128)}), f32[2,4,3840]{2,1,0:T(4,128)S(1)}, s32[]{:S(2)}) async-start(f32[2,4,4352]{2,1,0:T(4,128)} %param.5), calls=%async_computation.2 | async-start | bytes 245760 | tf_op jit(solution)/shard_map/slice | solution.py:81
  30.1 25.4 %all-to-all-start = ((f32[256,1,256]{2,1,0:T(1,128)}), f32[256,1,256]{2,1,0:T(1,128)}, u32[]{:S(2)}, u32[]{:S(2)}) async-start(f32[256,1,256]{2,1,0:T(1,128)} %all_to_all.16), calls=%async_computation | async-start | bytes 524288 | tf_op jit(solution)/shard_map/all_to_all | solution.py:155
  58.3 5.2 %copy-start.2 = (f32[512,256]{0,1:T(8,128)S(1)}, f32[512,256]{0,1:T(8,128)}, u32[]{:S(2)}) copy-start(f32[512,256]{0,1:T(8,128)} %fusion.2) | copy-start | bytes 1572868
  64.9 0.9 copy-start.3
  64.9 1.0 copy-start.4
  68.8 2.5 %copy-start = (f32[256,1280]{1,0:T(8,128)}, f32[256,1280]{1,0:T(8,128)S(1)}, u32[]{:S(2)}) copy-start(f32[256,1280]{1,0:T(8,128)S(1)} %get-tuple-element.15) | copy-start | bytes 3932164
  95.1 1.7 %copy-start.1 = (f32[2,8,16,1280]{3,2,1,0:T(8,128)S(1)}, f32[2,8,16,1280]{3,2,1,0:T(8,128)}, u32[]{:S(2)}) copy-start(f32[2,8,16,1280]{3,2,1,0:T(8,128)} %param.9) | copy-start | bytes 3932164
